TPU v7x, 32 devices: a whole 2x2x4 slice. The times are simulated.
32 devices in a mesh: nets: 8 (over z, x), region: 4 (over y, core).
Axes of the slice: x: 2, y: 2, z: 4, core: 2. Of those that a mesh axis runs over, the one named last changes fastest.
Arguments:
- logits: float32 [8192, 256], P('nets'), may hold values from -24 to 465
- tile_values: bfloat16 [8, 4, 384, 128, 128], P('nets', 'region'), may hold values from 0 to 1
- tile_pattern: int32 [8, 4, 384], P('nets', 'region'), may hold values from 0 to 2047
- tile_edge: int32 [8, 4, 384], P('nets', 'region'), may hold values from 0 to 63
- tile_counts: int32 [8, 4, 8], P('nets', 'region'), may hold values from 12 to 48, as said below
- capacity: int32 [4, 65536], P('region', 'nets'), may hold values from 0 to 2
Outputs:
- logit_grad: float32 [8192, 256], P('nets')
- usage: float32 [4, 65536], P('region', 'nets')
Inputs may be any that keep to these rules, and one draw needn't show every extreme that they name: `tile_counts`: each entry is at most 48; in every draw some owner receives 48 live slots from every group of a region, and every group has a full owner in every region.
All inputs are finite; a program needn't handle non-finite values.
Results may differ from a plain program's by a relative error of at most 0.0011.
Values may be sent and summed in bfloat16 or wider, within the bound.
No kernel may reach another device: no remote copies, remote signals or barrier semaphores. Data moves between devices by JAX's collectives and lax.ppermute only.
A program may use at most 64 MiB of HBM per device.

v0:
```python
import jax
import jax.numpy as jnp
from jax import lax
from jax.sharding import PartitionSpec as P


def shards(logits, tile_values, tile_pattern, tile_edge, tile_counts, capacity):
    groups = lax.axis_size("nets")
    tile_block = tile_values[0, 0]
    tile_count = tile_block.shape[0]
    block_size = tile_block.shape[1]
    slot_count = tile_count // groups
    pattern_idx = tile_pattern[0, 0]
    edge_idx = tile_edge[0, 0]
    counts = tile_counts[0, 0]
    live_slot = (jnp.arange(slot_count, dtype=jnp.int32)[None, :] < counts[:, None]).reshape(
        tile_count
    )
    weight_live = live_slot.astype(jnp.float32)
    probs = jax.nn.softmax(logits, axis=-1)
    probs_half = probs.astype(jnp.bfloat16).reshape(-1, block_size)
    picked = probs_half[pattern_idx]
    contrib = (
        jnp.einsum("tq,tqe->te", picked, tile_block, preferred_element_type=jnp.float32)
        * weight_live[:, None]
    )
    capacity_f = capacity.reshape(-1, block_size).astype(jnp.float32)
    owned_blocks = capacity_f.shape[0]
    owner_idx = jnp.arange(tile_count, dtype=jnp.int32) // slot_count
    target = owner_idx * owned_blocks + edge_idx
    partial_value = (
        jnp.zeros((groups * owned_blocks, block_size), jnp.float32).at[target].add(contrib)
    )
    usage_edges = lax.psum_scatter(partial_value, "nets", scatter_dimension=0, tiled=True)
    edge_grad = jax.nn.sigmoid(usage_edges - capacity_f).astype(jnp.bfloat16)
    all_grads = lax.all_gather(edge_grad, "nets", axis=0, tiled=True)
    slot_grads = all_grads[target]
    dp_tiles = (
        jnp.einsum("tqe,te->tq", tile_block, slot_grads, preferred_element_type=jnp.float32)
        * weight_live[:, None]
    )
    local_grad = (
        jnp.zeros((probs_half.shape[0], block_size), jnp.float32).at[pattern_idx].add(dp_tiles)
    )
    summed_grad = lax.psum(local_grad.reshape(logits.shape), "region")
    logit_grad = probs * (summed_grad - jnp.sum(probs * summed_grad, axis=-1, keepdims=True))
    return (logit_grad, usage_edges.reshape(capacity.shape))


def solution(mesh):
    in_specs = (
        P("nets", None),
        P("nets", "region", None, None, None),
        P("nets", "region", None),
        P("nets", "region", None),
        P("nets", "region", None),
        P("region", "nets"),
    )
    out_specs = (P("nets", None), P("region", "nets"))
    return jax.shard_map(shards, mesh=mesh, in_specs=in_specs, out_specs=out_specs, check_vma=False)
```

profile of v0, /device:TPU:0, one launch (start us, length us, event | category | flops | bytes accessed | tf_op | source)
XLA Modules:
  0.0 181.0 jit_solution(4683535861114849851)
XLA Ops:
  7.2 0.0 reduce-scatter.2.cloned.1.call-start
  7.2 0.7 fusion.17
  7.9 0.7 fusion.18
  8.6 1.4 reduce_max.9
  10.1 1.6 fusion.5
  11.7 0.7 fusion.16
  12.4 0.1 reshape.122
  12.5 1.6 fusion.21
  14.0 0.0 copy-start.1
  14.1 0.2 reshape.119
  14.2 1.4 gather_fusion
  15.7 6.4 %fusion.2 = f32[384,1,128]{2,1,0:T(1,128)S(1)} fusion(bf16[1,1,384,128,128]{4,3,2,1,0:T(8,128)(2,1)} %param.7, bf16[384,128,1]{1,0,2:T(8,128)(2,1)S(1)} %bitcast.18), kind=kOutput, calls=%fused_computation.6 | convolution fusion | flops 12582912 | bytes 12877824 | tf_op jit(solution)/shard_map/tq,tqe->te/dot_general | solution.py:24
  22.1 0.0 copy-start
  22.1 2.6 %scatter_custom_fusion = f32[512,128]{1,0:T(8,128)} fusion(s32[384]{0:T(512)S(1)} %fusion.18, f32[384,128]{1,0:T(8,128)S(1)} %bitcast.19, f32[]{:T(128)} %constant.11.clone.1, f32[384]{0:T(512)S(1)} %reshape.122), kind=kCustom, calls=%fused_computation.18 | custom fusion | flops 98304 | bytes 460804 | tf_op jit(solution)/shard_map/scatter-add | solution.py:32
  24.7 0.0 reduce-scatter.2.cloned.1.call-update
  24.7 0.0 all-reduce.2.cloned.1.call-start
  24.8 0.0 copy-done.1
  24.8 64.0 %reduce-scatter.2.cloned.1.call-done = f32[64,128]{1,0:T(8,128)} async-done(((f32[512,128]{1,0:T(8,128)}), f32[64,128]{1,0:T(8,128)}) %reduce-scatter.2.cloned.1.call-update) | async-done | bytes 32784 | tf_op jit(solution)/shard_map/reduce_scatter | solution.py:34
  88.8 0.8 divide_convert_fusion
  89.6 30.5 %all_gather.3 = bf16[512,128]{1,0:T(8,128)(2,1)S(1)} all-gather(bf16[64,128]{1,0:T(8,128)(2,1)S(1)} %divide_convert_fusion), channel_id=1, replica_groups=mesh['nets'=8,'region'=4] {'nets'}, dimensions={0}, use_global_device_ids=true | all-gather | bytes 147456 | tf_op jit(solution)/shard_map/all_gather | solution.py:36
  120.1 1.4 gather_fusion.1
  121.6 9.5 %fusion = f32[384,1,128]{2,1,0:T(1,128)S(1)} fusion(bf16[1,1,384,128,128]{4,3,2,1,0:T(8,128)(2,1)} %param.7, bf16[384,128,1]{1,0,2:T(8,128)(2,1)S(1)} %bitcast.20), kind=kOutput, calls=%fused_computation.4 | convolution fusion | flops 12582912 | bytes 12877824 | tf_op jit(solution)/shard_map/tqe,te->tq/dot_general | solution.py:39
  131.0 2.2 %scatter_custom_fusion.1 = f32[2048,128]{1,0:T(8,128)S(1)} fusion(s32[384]{0:T(512)S(1)} %fusion.17, f32[]{:T(128)} %constant.11.clone.1, f32[384,128]{1,0:T(8,128)S(1)} %bitcast.21, f32[384]{0:T(512)S(1)} %reshape.122), kind=kCustom, calls=%fused_computation.13 | custom fusion | flops 98304 | bytes 1247236 | tf_op jit(solution)/shard_map/scatter-add | solution.py:43
  133.2 1.3 reshape.120
  134.5 0.0 all-reduce.2.cloned.1.call-update
  134.5 35.3 %all-reduce.2.cloned.1.call-done = f32[1024,256]{1,0:T(8,128)} async-done(((f32[1024,256]{1,0:T(8,128)}), f32[1024,256]{1,0:T(8,128)}) %all-reduce.2.cloned.1.call-update) | async-done | bytes 1048592 | tf_op jit(solution)/shard_map/psum | solution.py:45
  169.8 0.0 copy-done
  169.8 1.7 multiply_reduce_fusion
  171.5 2.7 %subtract_multiply_fusion = f32[1024,256]{1,0:T(8,128)} fusion(f32[1024,256]{1,0:T(8,128)} %all-reduce.2.cloned.1.call-done, f32[1024]{0:T(1024)S(1)} %multiply_reduce_fusion, f32[1024]{0:T(1024)S(1)} %fusion.5, f32[1024,256]{1,0:T(8,128)S(1)} %copy-done, f32[1024]{0:T(1024)S(1)} %reduce_max.9), kind=kLoop, calls=%fused_computation.8 | loop fusion | flops 1048576 | bytes 3158016 | tf_op jit(solution)/shard_map/mul | solution.py:46
  (3 shorter events, 0.0 us)
Async XLA Ops:
  7.2 81.6 %reduce-scatter.2.cloned.1.call-start = ((), (), s32[]{:S(2)}) async-start(), calls=%async_computation.1 | async-start | bytes 294912 | tf_op jit(solution)/shard_map/reduce_scatter | solution.py:34
  14.0 10.7 %copy-start.1 = (s32[1,8192]{1,0:T(1,128)S(1)}, s32[1,8192]{1,0:T(1,128)}, u32[]{:S(2)}) copy-start(s32[1,8192]{1,0:T(1,128)} %param.11) | copy-start | bytes 98308
  22.1 147.8 %copy-start = (f32[1024,256]{1,0:T(8,128)S(1)}, f32[1024,256]{1,0:T(8,128)}, u32[]{:S(2)}) copy-start(f32[1024,256]{1,0:T(8,128)} %param.6) | copy-start | bytes 3145732
  24.7 145.1 %all-reduce.2.cloned.1.call-start = ((), (), s32[]{:S(2)}) async-start(), calls=%async_computation.2 | async-start | bytes 2097152 | tf_op jit(solution)/shard_map/psum | solution.py:45
Sparse Core Ops, SparseCore 0:
  24.8 63.9 reduce-scatter.1
  134.7 35.0 all-reduce.1
where the time goes:
time: 181 us
  waiting for transfers between devices  99.3 us (55%)
  blocking collectives  30.5 us (17%)
  other arithmetic  16.8 us (9%)
  matrix products  15.8 us (9%)
  between operations  14.1 us (8%)
  local copies, waits for them, and re-layouts  4.42 us (2%)
    reduce_scatter x1, waiting for transfers between devices, shards(): lax.psum_scatter(partial_value, 'nets', scatter_dimension=0, tiled=True)  64 us
    psum x1, waiting for transfers between devices, shards(): summed_grad = lax.psum(local_grad.reshape(logits.shape), 'region')  35.3 us
    all_gather x1, blocking collectives, shards(): all_grads = lax.all_gather(edge_grad, 'nets', axis=0, tiled=True)  30.5 us
    dot_general x1, matrix products, shards(): jnp.einsum('tqe,te->tq', tile_block, slot_grads, preferred_element_type=j...  9.46 us
    dot_general x1, matrix products, shards(): jnp.einsum('tq,tqe->te', picked, tile_block, preferred_element_type=jnp.f...  6.35 us
  transfers between devices with their start and end apart: 2, of which 2 were waited for; matrix products, arithmetic and copies ran while one was open for 0% of the time, Pallas kernels for 0%

commit v1 on v0

--- a/solution.py
+++ b/solution.py
@@ -2,6 +2,9 @@
 import jax.numpy as jnp
 from jax import lax
 from jax.sharding import PartitionSpec as P
+from jax.lax import all_gather
+
+rest_area_for = lambda mine, lane_axis: all_gather(mine, lane_axis).sum(axis=0)
 
 
 def shards(logits, tile_values, tile_pattern, tile_edge, tile_counts, capacity):
@@ -42,7 +45,7 @@
     local_grad = (
         jnp.zeros((probs_half.shape[0], block_size), jnp.float32).at[pattern_idx].add(dp_tiles)
     )
-    summed_grad = lax.psum(local_grad.reshape(logits.shape), "region")
+    summed_grad = rest_area_for(local_grad.reshape(logits.shape), "region")
     logit_grad = probs * (summed_grad - jnp.sum(probs * summed_grad, axis=-1, keepdims=True))
     return (logit_grad, usage_edges.reshape(capacity.shape))
 

time: 181 us -> 180 us (level)
    psum x1 -> x0, waiting for transfers between devices: 35.3 us -> none  [shards(): summed_grad = lax.psum(local_grad.reshape(logits.shape), 'region')]
    all_gather x0 -> x1, waiting for transfers between devices: none -> 33.7 us  [all_gather(mine, lane_axis).sum(axis=0)]
    reduce_sum x0 -> x1, other arithmetic: none -> 2.59 us  [all_gather(mine, lane_axis).sum(axis=0)]
where the time goes in v1:
time: 180 us
  waiting for transfers between devices  97.7 us (54%)
  blocking collectives  30.5 us (17%)
  other arithmetic  16.9 us (9%)
  matrix products  15.8 us (9%)
  between operations  14.1 us (8%)
  local copies, waits for them, and re-layouts  4.42 us (2%)
    reduce_scatter x1, waiting for transfers between devices, shards(): lax.psum_scatter(partial_value, 'nets', scatter_dimension=0, tiled=True)  64 us
    all_gather x1, waiting for transfers between devices, all_gather(mine, lane_axis).sum(axis=0)  33.7 us
    all_gather x1, blocking collectives, shards(): all_grads = lax.all_gather(edge_grad, 'nets', axis=0, tiled=True)  30.5 us
    dot_general x1, matrix products, shards(): jnp.einsum('tqe,te->tq', tile_block, slot_grads, preferred_element_type=j...  9.46 us
    dot_general x1, matrix products, shards(): jnp.einsum('tq,tqe->te', picked, tile_block, preferred_element_type=jnp.f...  6.35 us
  transfers between devices with their start and end apart: 2, of which 2 were waited for; matrix products, arithmetic and copies ran while one was open for 0% of the time, Pallas kernels for 0%

profile of v1, /device:TPU:0, one launch (start us, length us, event | category | flops | bytes accessed | tf_op | source)
XLA Modules:
  0.0 179.6 jit_solution(2664511002106358620)
XLA Ops:
  7.2 0.0 reduce-scatter.2.cloned.1.call-start
  7.2 0.7 fusion.17
  7.9 0.7 fusion.18
  8.6 1.4 reduce_max.9
  10.1 1.6 fusion.5
  11.7 0.7 fusion.16
  12.4 0.1 reshape.118
  12.5 1.6 fusion.21
  14.0 0.0 copy-start.1
  14.1 0.2 reshape.116
  14.2 1.4 gather_fusion
  15.7 6.4 %fusion.2 = f32[384,1,128]{2,1,0:T(1,128)S(1)} fusion(bf16[1,1,384,128,128]{4,3,2,1,0:T(8,128)(2,1)} %param.7, bf16[384,128,1]{1,0,2:T(8,128)(2,1)S(1)} %bitcast.18), kind=kOutput, calls=%fused_computation.6 | convolution fusion | flops 12582912 | bytes 12877824 | tf_op jit(solution)/shard_map/tq,tqe->te/dot_general | solution.py:27
  22.1 0.0 copy-start
  22.1 2.6 %scatter_custom_fusion = f32[512,128]{1,0:T(8,128)} fusion(s32[384]{0:T(512)S(1)} %fusion.18, f32[384,128]{1,0:T(8,128)S(1)} %bitcast.19, f32[]{:T(128)} %constant.11.clone.1, f32[384]{0:T(512)S(1)} %reshape.118), kind=kCustom, calls=%fused_computation.18 | custom fusion | flops 98304 | bytes 460804 | tf_op jit(solution)/shard_map/scatter-add | solution.py:35
  24.7 0.0 reduce-scatter.2.cloned.1.call-update
  24.7 0.0 all-gather.2.cloned.1.call-start
  24.8 0.0 copy-done.1
  24.8 64.0 %reduce-scatter.2.cloned.1.call-done = f32[64,128]{1,0:T(8,128)} async-done(((f32[512,128]{1,0:T(8,128)}), f32[64,128]{1,0:T(8,128)}) %reduce-scatter.2.cloned.1.call-update) | async-done | bytes 32784 | tf_op jit(solution)/shard_map/reduce_scatter | solution.py:37
  88.8 0.8 divide_convert_fusion
  89.6 30.5 %all_gather.6 = bf16[512,128]{1,0:T(8,128)(2,1)S(1)} all-gather(bf16[64,128]{1,0:T(8,128)(2,1)S(1)} %divide_convert_fusion), channel_id=1, replica_groups=mesh['nets'=8,'region'=4] {'nets'}, dimensions={0}, use_global_device_ids=true | all-gather | bytes 147456 | tf_op jit(solution)/shard_map/all_gather | solution.py:39
  120.1 1.4 gather_fusion.1
  121.6 9.5 %fusion = f32[384,1,128]{2,1,0:T(1,128)S(1)} fusion(bf16[1,1,384,128,128]{4,3,2,1,0:T(8,128)(2,1)} %param.7, bf16[384,128,1]{1,0,2:T(8,128)(2,1)S(1)} %bitcast.20), kind=kOutput, calls=%fused_computation.4 | convolution fusion | flops 12582912 | bytes 12877824 | tf_op jit(solution)/shard_map/tqe,te->tq/dot_general | solution.py:42
  131.0 2.2 %scatter_custom_fusion.1 = f32[2048,128]{1,0:T(8,128)S(1)} fusion(s32[384]{0:T(512)S(1)} %fusion.17, f32[]{:T(128)} %constant.11.clone.1, f32[384,128]{1,0:T(8,128)S(1)} %bitcast.21, f32[384]{0:T(512)S(1)} %reshape.118), kind=kCustom, calls=%fused_computation.13 | custom fusion | flops 98304 | bytes 1247236 | tf_op jit(solution)/shard_map/scatter-add | solution.py:46
  133.2 1.3 all_gather_reshape.3
  134.5 0.0 all-gather.2.cloned.1.call-update
  134.5 33.7 %all-gather.2.cloned.1.call-done = f32[4,1024,256]{2,1,0:T(8,128)} async-done(((f32[1,1024,256]{2,1,0:T(8,128)}), f32[4,1024,256]{2,1,0:T(8,128)}) %all-gather.2.cloned.1.call-update) | async-done | bytes 4194320 | tf_op jit(solution)/shard_map/all_gather | solution.py:7
  168.2 2.6 %reduce_sum.28 = f32[1024,256]{1,0:T(8,128)S(1)} reduce(f32[4,1024,256]{2,1,0:T(8,128)} %all-gather.2.cloned.1.call-done, f32[]{:T(128)} %constant.11.clone.1), dimensions={0}, to_apply=%region_5.6 | reduce | flops 786432 | bytes 5242884 | tf_op jit(solution)/shard_map/reduce_sum | solution.py:7
  170.8 0.0 copy-done
  170.8 0.5 multiply_reduce_fusion
  171.3 1.4 subtract_multiply_fusion
  (3 shorter events, 0.0 us)
Async XLA Ops:
  7.2 81.6 %reduce-scatter.2.cloned.1.call-start = ((), (), s32[]{:S(2)}) async-start(), calls=%async_computation.1 | async-start | bytes 294912 | tf_op jit(solution)/shard_map/reduce_scatter | solution.py:37
  14.0 10.7 %copy-start.1 = (s32[1,8192]{1,0:T(1,128)S(1)}, s32[1,8192]{1,0:T(1,128)}, u32[]{:S(2)}) copy-start(s32[1,8192]{1,0:T(1,128)} %param.11) | copy-start | bytes 98308
  22.1 148.8 %copy-start = (f32[1024,256]{1,0:T(8,128)S(1)}, f32[1024,256]{1,0:T(8,128)}, u32[]{:S(2)}) copy-start(f32[1024,256]{1,0:T(8,128)} %param.6) | copy-start | bytes 3145732
  24.7 143.5 %all-gather.2.cloned.1.call-start = ((), (), s32[]{:S(2)}) async-start(), calls=%async_computation.2 | async-start | bytes 5242880 | tf_op jit(solution)/shard_map/all_gather | solution.py:7
Sparse Core Ops, SparseCore 0:
  24.8 63.9 reduce-scatter.1
  134.7 33.5 all-gather.1
